TPU v7x, 32 devices: a whole 2x2x4 slice. The times are simulated.
32 devices in a mesh: species: 4 (over z), space: 8 (over y, x, core).
Axes of the slice: x: 2, y: 2, z: 4, core: 2. Of those that a mesh axis runs over, the one named last changes fastest.
Arguments:
- density: float32 [4, 32, 16, 32, 128], P('species', None, 'space'), may hold values from 0 to 2
- space_factor: float32 [16, 32, 128], P('space'), may hold values from 0.5 to 1
- diff_rate: float32 [4, 32], P('species'), may hold values from 0.02 to 0.08
- loss_inverse: float32 [4, 32, 32], P('species'), may hold values from 0 to 1, as said below
- chain_yield: float32 [4, 32], P('species'), may hold values from 0.25 to 0.95
- survival: float32 [4, 32], P('species'), may hold values from 0.6 to 1
- gamma_yield: float32 [4, 32], P('species'), may hold values from 0.1 to 1
- sky_weight: bfloat16 [8, 8, 64, 128], P('space'), may hold values from -0.75 to 0.75
- sky_blocks: int32 [8, 8], P('space'), may hold values from 0 to 383
Outputs:
- propagated: float32 [4, 32, 16, 32, 128], P('species', None, 'space')
- sky: float32 [384, 128], P('space')
Inputs may be any that keep to these rules, and one draw needn't show every extreme that they name: `loss_inverse`: each matrix is upper triangular with a diagonal of 0.5 to 1 and nonnegative entries.
All inputs are finite; a program needn't handle non-finite values.
Results may differ from a plain program's by a relative error of at most 0.0011.
Values sent between devices are 32-bit elements; how exact they have to be, the bound alone decides.
No kernel may reach another device: no remote copies, remote signals or barrier semaphores. Data moves between devices by JAX's collectives and lax.ppermute only.
A program may use at most 64 MiB of HBM per device.

v0:
```python
import jax
import jax.numpy as jnp
from jax import lax
from jax.sharding import PartitionSpec as P

SUBSTEPS = 2
NB = 384
HIGH = lax.Precision.HIGHEST


def padded_2(cells, sides, width):
    for axis, dim in sides:
        count = lax.axis_size(axis)
        ends = count - 1
        head = lax.slice_in_dim(cells, 0, width, axis=dim)
        tail = lax.slice_in_dim(cells, cells.shape[dim] - width, cells.shape[dim], axis=dim)
        cells = jnp.concatenate(
            [
                lax.ppermute(tail, axis, [(i, (i + 1) % count) for i in range(ends)]),
                cells,
                lax.ppermute(head, axis, [((i + 1) % count, i) for i in range(ends)]),
            ],
            axis=dim,
        )
    return cells


def from_behind(block, axis, distance):
    devices = range(lax.axis_size(axis))
    route = [(i - distance, i) for i in devices if i - distance in devices]
    return lax.ppermute(block, axis, route)


def cross_sum(field):
    padded = jnp.pad(field, ((0, 0), (0, 0), (1, 1), (1, 1)))
    beside = padded[:, :, 2:, 1:-1] + padded[:, :, :-2, 1:-1]
    beside = beside + padded[:, :, 1:-1, 2:] + padded[:, :, 1:-1, :-2]
    return beside


def emission_weights(chain_all, gamma_all, me):
    groups = chain_all.shape[0]
    g = jnp.arange(groups)[:, None]
    k = jnp.arange(groups)[None, :]
    live = (k > me) & (k <= g)
    factors = jnp.where(live[:, :, None], chain_all[None, :, :], 1.0)
    spread = jnp.prod(factors, axis=1)
    return jnp.where(g >= me, gamma_all * spread, 0.0)


def body(
    density,
    space_factor,
    diff_rate,
    loss_inverse,
    chain_yield,
    survival,
    gamma_yield,
    sky_weight,
    sky_blocks,
):
    tiles = lax.axis_size("space")
    rows = NB // tiles
    params = jnp.stack([chain_yield[0], gamma_yield[0]])
    params_all = lax.all_gather(params, "species")
    blocks_all = lax.all_gather(sky_blocks[0].astype(jnp.float32), "space")
    field = density[0]
    bins = field.shape[0]
    width = field.shape[1]
    depth = field.shape[3]
    rate = diff_rate[0][:, None, None, None]
    factor = rate * space_factor[None]
    for step in range(SUBSTEPS):
        wider = padded_2(field, (("space", 1),), 1)
        beside = wider[:, 2:] + wider[:, :-2] + cross_sum(field)
        field = field + factor * (beside - 6.0 * field)
    solved = jnp.dot(
        loss_inverse[0], field.reshape(bins, -1), precision=HIGH, preferred_element_type=jnp.float32
    ).reshape(field.shape)
    factor_chain = chain_yield[0][:, None, None, None]
    own_part = survival[0][:, None, None, None] * solved
    me = lax.axis_index("species")
    weights = emission_weights(params_all[:, 0], params_all[:, 1], me)
    own_columns = jnp.sum(own_part, axis=3).reshape(bins, -1)
    partial = jnp.dot(weights, own_columns, precision=HIGH, preferred_element_type=jnp.float32)
    sums = lax.psum(partial, "species")
    emission = (sums / (bins * depth)).astype(jnp.bfloat16).astype(jnp.float32)
    columns = jnp.sum(emission, axis=0)
    contribution = jnp.einsum(
        "c,lcb->lb", columns, sky_weight[0].astype(jnp.float32), precision=HIGH
    )
    gathered = lax.all_gather(contribution, "space")
    lines = gathered.shape[1]
    mine = lax.axis_index("space") * rows + jnp.arange(rows, dtype=jnp.int32)
    onehot = (blocks_all.reshape(1, tiles * lines) == mine.astype(jnp.float32)[:, None]).astype(
        jnp.float32
    )
    sky = jnp.dot(
        onehot,
        gathered.reshape(tiles * lines, -1),
        precision=HIGH,
        preferred_element_type=jnp.float32,
    )
    carried = own_part
    for section in range(lax.axis_size("species") - 1):
        carried = factor_chain * from_behind(carried, "species", 1) + own_part
    return (carried[None], sky)


def solution(mesh):
    placed = (
        P("species", None, "space", None, None),
        P("space", None, None),
        P("species", None),
        P("species", None, None),
        P("species", None),
        P("species", None),
        P("species", None),
        P("space", None, None, None),
        P("space", None),
    )
    return jax.shard_map(
        body,
        mesh=mesh,
        in_specs=placed,
        out_specs=(P("species", None, "space", None, None), P("space", None)),
        check_vma=False,
    )
```

profile of v0, /device:TPU:0, one launch (start us, length us, event | category | flops | bytes accessed | tf_op | source)
XLA Modules:
  0.0 139.3 jit_solution(8967124272913731241)
XLA Ops:
  0.6 0.0 copy-start
  0.6 0.0 copy-start.1
  0.7 0.0 copy-start.2
  0.7 0.0 copy-start.5
  0.7 1.4 fusion.34
  2.0 1.3 collective-permute-start
  3.4 3.1 %collective-permute-start.1 = (f32[32,1,32,128]{3,2,1,0:T(8,128)S(1)}, f32[32,1,32,128]{3,2,1,0:T(8,128)S(1)}, u32[]{:S(2)}, u32[]{:S(2)}) collective-permute-start(f32[32,1,32,128]{3,2,1,0:T(8,128)S(1)} %get-tuple-element.7), channel_id=1, source_target_pairs={{0,1},{1,2},{2,3},{3,4},{4,5},{5,6},{6,7},{8,9},{9,10},{10,11},{11... | collective-permute-start | bytes 1572872 | tf_op jit(solution)/shard_map/ppermute | solution.py:19
  6.4 0.0 collective-permute-done
  6.4 1.5 %collective-permute-done.1 = f32[32,1,32,128]{3,2,1,0:T(8,128)S(1)} collective-permute-done((f32[32,1,32,128]{3,2,1,0:T(8,128)S(1)}, f32[32,1,32,128]{3,2,1,0:T(8,128)S(1)}, u32[]{:S(2)}, u32[]{:S(2)}) %collective-permute-start.1) | collective-permute-done | bytes 524320 | tf_op jit(solution)/shard_map/ppermute | solution.py:19
  7.9 0.0 copy-done.1
  7.9 0.0 copy-done.2
  7.9 0.0 copy-done.5
  7.9 0.8 fusion
  8.7 0.1 fusion.33
  8.8 1.3 collective-permute-start.2
  10.1 0.0 copy-start.3
  10.1 10.4 %collective-permute-start.3 = (f32[32,1,32,128]{3,2,1,0:T(8,128)S(1)}, f32[32,1,32,128]{3,2,1,0:T(8,128)S(1)}, u32[]{:S(2)}, u32[]{:S(2)}) collective-permute-start(f32[32,1,32,128]{3,2,1,0:T(8,128)S(1)} %get-tuple-element.5), channel_id=1, source_target_pairs={{0,1},{1,2},{2,3},{3,4},{4,5},{5,6},{6,7},{8,9},{9,10},{10,11},{11... | collective-permute-start | bytes 1572872 | tf_op jit(solution)/shard_map/ppermute | solution.py:19
  20.5 0.0 collective-permute-done.2
  20.5 1.5 %collective-permute-done.3 = f32[32,1,32,128]{3,2,1,0:T(8,128)S(1)} collective-permute-done((f32[32,1,32,128]{3,2,1,0:T(8,128)S(1)}, f32[32,1,32,128]{3,2,1,0:T(8,128)S(1)}, u32[]{:S(2)}, u32[]{:S(2)}) %collective-permute-start.3) | collective-permute-done | bytes 524320 | tf_op jit(solution)/shard_map/ppermute | solution.py:19
  22.0 0.8 fusion.1
  22.8 0.0 copy-done.3
  22.8 1.7 %convolution_bitcast_fusion = f32[4,8,64,128]{3,1,2,0:T(8,128)S(1)} fusion(f32[4,8,64,128]{3,2,1,0:T(8,128)S(1)} %bitcast.49, f32[1,32,32]{2,1,0:T(8,128)S(1)} %copy-done.3), kind=kOutput, calls=%fused_computation.10 | convolution fusion | flops 100663296 | bytes 2101248 | tf_op jit(solution)/shard_map/dot_general | solution.py:77
  24.5 0.0 copy-start.6
  24.5 0.2 copy.17
  24.7 0.5 copy-done.6
  25.2 0.0 copy-start.4
  25.2 0.5 fusion.32
  25.7 3.6 %collective-permute-start.4 = (f32[32,2,32,128]{3,2,1,0:T(8,128)S(1)}, f32[32,2,32,128]{3,2,1,0:T(8,128)S(1)}, u32[]{:S(2)}, u32[]{:S(2)}) collective-permute-start(f32[32,2,32,128]{3,2,1,0:T(8,128)S(1)} %get-tuple-element.3), channel_id=1, source_target_pairs={{0,8},{8,16},{16,24},{1,9},{9,17},{17,25},{2,10},{10,18},{18,26},{... | collective-permute-start | bytes 3145736 | tf_op jit(solution)/shard_map/ppermute | solution.py:31
  29.2 18.0 %collective-permute-done.4 = f32[32,2,32,128]{3,2,1,0:T(8,128)S(1)} collective-permute-done((f32[32,2,32,128]{3,2,1,0:T(8,128)S(1)}, f32[32,2,32,128]{3,2,1,0:T(8,128)S(1)}, u32[]{:S(2)}, u32[]{:S(2)}) %collective-permute-start.4) | collective-permute-done | bytes 1048608 | tf_op jit(solution)/shard_map/ppermute | solution.py:31
  47.2 0.0 copy-done.4
  47.2 0.0 copy-start.7
  47.2 0.0 copy-start.8
  47.2 0.2 multiply_add_fusion.1
  47.5 5.4 %collective-permute-start.5 = (f32[32,2,32,128]{3,2,1,0:T(8,128)S(1)}, f32[32,2,32,128]{3,2,1,0:T(8,128)}, u32[]{:S(2)}, u32[]{:S(2)}) collective-permute-start(f32[32,2,32,128]{3,2,1,0:T(8,128)S(1)} %multiply_add_fusion.1), channel_id=1, source_target_pairs={{0,8},{8,16},{16,24},{1,9},{9,17},{17,25},{2,10},{10,18},{18,26},{... | collective-permute-start | bytes 3145736 | tf_op jit(solution)/shard_map/ppermute | solution.py:31
  52.8 0.0 copy-done.7
  52.8 24.3 %all-gather.3 = f32[4,2,32]{2,1,0:T(2,128)S(1)} all-gather(f32[1,2,32]{2,1,0:T(2,128)S(1)} %maximum_bitcast_fusion), channel_id=2, replica_groups=mesh['species'=4,'space'=8] {'species'}, dimensions={0}, use_global_device_ids=true | all-gather | bytes 1280 | tf_op jit(solution)/shard_map/all_gather | solution.py:65
  77.2 0.0 copy-done.8
  77.2 0.0 collective-permute-done.5
  77.2 1.4 multiply_add_fusion
  78.6 1.4 collective-permute-start.6
  80.0 29.6 %all-gather.2 = f32[8,1,8]{2,1,0:T(1,128)S(1)} all-gather(f32[1,1,8]{2,1,0:T(1,128)S(1)} %convert_bitcast_fusion), channel_id=1, replica_groups=mesh['species'=4,'space'=8] {'space'}, dimensions={0}, use_global_device_ids=true | all-gather | bytes 288 | tf_op jit(solution)/shard_map/all_gather | solution.py:66
  109.6 0.5 broadcast.46
  110.1 0.7 reduce.3
  110.8 0.1 eq.15
  110.9 0.1 select_reduce_fusion
  111.0 0.1 reshape.73
  111.0 0.2 fusion.23
  111.2 8.9 %psum.7 = f32[4,64]{1,0:T(4,128)S(1)} all-reduce(f32[4,64]{1,0:T(4,128)S(1)} %fusion.23), channel_id=1, replica_groups=mesh['species'=4,'space'=8] {'species'}, use_global_device_ids=true, to_apply=%region_2.3 | all-reduce | flops 256 | bytes 2048 | tf_op jit(solution)/shard_map/psum | solution.py:86
  120.2 0.0 copy-done
  120.2 0.2 fusion.16
  120.3 17.1 %all-gather.1 = f32[64,128]{1,0:T(8,128)S(1)} all-gather(f32[8,128]{1,0:T(8,128)S(1)} %bitcast.50), channel_id=3, replica_groups=mesh['species'=4,'space'=8] {'space'}, dimensions={0}, use_global_device_ids=true | all-gather | bytes 36864 | tf_op jit(solution)/shard_map/all_gather | solution.py:92
  137.4 0.8 fusion.18
  138.2 0.0 collective-permute-done.6
  138.2 1.1 add_bitcast_fusion
  (8 shorter events, 0.1 us)
Async XLA Ops:
  0.6 119.5 %copy-start = (bf16[1,8,64,128]{3,2,1,0:T(8,128)(2,1)S(1)}, bf16[1,8,64,128]{3,2,1,0:T(8,128)(2,1)}, u32[]{:S(2)}) copy-start(bf16[1,8,64,128]{3,2,1,0:T(8,128)(2,1)} %param.16) | copy-start | bytes 393220
  0.6 7.3 %copy-start.1 = (f32[1,32,2,32,128]{4,3,2,1,0:T(8,128)S(1)}, f32[1,32,2,32,128]{4,3,2,1,0:T(8,128)}, u32[]{:S(2)}) copy-start(f32[1,32,2,32,128]{4,3,2,1,0:T(8,128)} %param.9) | copy-start | bytes 3145732
  0.7 7.3 %copy-start.2 = (f32[2,32,128]{2,1,0:T(8,128)S(1)}, f32[2,32,128]{2,1,0:T(8,128)}, u32[]{:S(2)}) copy-start(f32[2,32,128]{2,1,0:T(8,128)} %param.10) | copy-start | bytes 98308
  0.7 7.2 %copy-start.5 = (f32[1,32]{1,0:T(1,128)S(1)}, f32[1,32]{1,0:T(1,128)}, u32[]{:S(2)}) copy-start(f32[1,32]{1,0:T(1,128)} %param.11) | copy-start | bytes 388
  2.0 4.4 %collective-permute-start = (f32[32,1,32,128]{3,2,1,0:T(8,128)S(1)}, f32[32,1,32,128]{3,2,1,0:T(8,128)S(1)}, u32[]{:S(2)}, u32[]{:S(2)}) collective-permute-start(f32[32,1,32,128]{3,2,1,0:T(8,128)S(1)} %get-tuple-element.6), channel_id=1, source_target_pairs={{1,0},{2,1},{3,2},{4,3},{5,4},{6,5},{7,6},{9,8},{10,9},{11,10},{12... | collective-permute-start | bytes 1572872 | tf_op jit(solution)/shard_map/ppermute | solution.py:21
  3.4 4.6 %collective-permute-start.1 = (f32[32,1,32,128]{3,2,1,0:T(8,128)S(1)}, f32[32,1,32,128]{3,2,1,0:T(8,128)S(1)}, u32[]{:S(2)}, u32[]{:S(2)}) collective-permute-start(f32[32,1,32,128]{3,2,1,0:T(8,128)S(1)} %get-tuple-element.7), channel_id=1, source_target_pairs={{0,1},{1,2},{2,3},{3,4},{4,5},{5,6},{6,7},{8,9},{9,10},{10,11},{11... | collective-permute-start | bytes 1572872 | tf_op jit(solution)/shard_map/ppermute | solution.py:19
  8.8 11.7 %collective-permute-start.2 = (f32[32,1,32,128]{3,2,1,0:T(8,128)S(1)}, f32[32,1,32,128]{3,2,1,0:T(8,128)S(1)}, u32[]{:S(2)}, u32[]{:S(2)}) collective-permute-start(f32[32,1,32,128]{3,2,1,0:T(8,128)S(1)} %get-tuple-element.4), channel_id=1, source_target_pairs={{1,0},{2,1},{3,2},{4,3},{5,4},{6,5},{7,6},{9,8},{10,9},{11,10},{12... | collective-permute-start | bytes 1572872 | tf_op jit(solution)/shard_map/ppermute | solution.py:21
  10.1 12.7 %copy-start.3 = (f32[1,32,32]{2,1,0:T(8,128)S(1)}, f32[1,32,32]{2,1,0:T(8,128)}, u32[]{:S(2)}) copy-start(f32[1,32,32]{2,1,0:T(8,128)} %param.12) | copy-start | bytes 12292
  10.1 11.9 %collective-permute-start.3 = (f32[32,1,32,128]{3,2,1,0:T(8,128)S(1)}, f32[32,1,32,128]{3,2,1,0:T(8,128)S(1)}, u32[]{:S(2)}, u32[]{:S(2)}) collective-permute-start(f32[32,1,32,128]{3,2,1,0:T(8,128)S(1)} %get-tuple-element.5), channel_id=1, source_target_pairs={{0,1},{1,2},{2,3},{3,4},{4,5},{5,6},{6,7},{8,9},{9,10},{10,11},{11... | collective-permute-start | bytes 1572872 | tf_op jit(solution)/shard_map/ppermute | solution.py:19
  24.5 0.7 copy-start.6
  25.2 22.0 %copy-start.4 = (f32[1,32]{1,0:T(1,128)S(1)}, f32[1,32]{1,0:T(1,128)}, u32[]{:S(2)}) copy-start(f32[1,32]{1,0:T(1,128)} %param.13) | copy-start | bytes 388
  25.7 21.5 %collective-permute-start.4 = (f32[32,2,32,128]{3,2,1,0:T(8,128)S(1)}, f32[32,2,32,128]{3,2,1,0:T(8,128)S(1)}, u32[]{:S(2)}, u32[]{:S(2)}) collective-permute-start(f32[32,2,32,128]{3,2,1,0:T(8,128)S(1)} %get-tuple-element.3), channel_id=1, source_target_pairs={{0,8},{8,16},{16,24},{1,9},{9,17},{17,25},{2,10},{10,18},{18,26},{... | collective-permute-start | bytes 3145736 | tf_op jit(solution)/shard_map/ppermute | solution.py:31
  47.2 5.6 %copy-start.7 = (f32[1,32]{1,0:T(1,128)S(1)}, f32[1,32]{1,0:T(1,128)}, u32[]{:S(2)}) copy-start(f32[1,32]{1,0:T(1,128)} %param.15) | copy-start | bytes 388
  47.2 30.0 %copy-start.8 = (s32[1,8]{1,0:T(1,128)S(1)}, s32[1,8]{1,0:T(1,128)}, u32[]{:S(2)}) copy-start(s32[1,8]{1,0:T(1,128)} %param.17) | copy-start | bytes 100
  47.5 29.7 %collective-permute-start.5 = (f32[32,2,32,128]{3,2,1,0:T(8,128)S(1)}, f32[32,2,32,128]{3,2,1,0:T(8,128)}, u32[]{:S(2)}, u32[]{:S(2)}) collective-permute-start(f32[32,2,32,128]{3,2,1,0:T(8,128)S(1)} %multiply_add_fusion.1), channel_id=1, source_target_pairs={{0,8},{8,16},{16,24},{1,9},{9,17},{17,25},{2,10},{10,18},{18,26},{... | collective-permute-start | bytes 3145736 | tf_op jit(solution)/shard_map/ppermute | solution.py:31
  78.6 59.6 %collective-permute-start.6 = (f32[32,2,32,128]{3,2,1,0:T(8,128)S(1)}, f32[32,2,32,128]{3,2,1,0:T(8,128)S(1)}, u32[]{:S(2)}, u32[]{:S(2)}) collective-permute-start(f32[32,2,32,128]{3,2,1,0:T(8,128)S(1)} %multiply_add_fusion), channel_id=1, source_target_pairs={{0,8},{8,16},{16,24},{1,9},{9,17},{17,25},{2,10},{10,18},{18,26},{... | collective-permute-start | bytes 3145736 | tf_op jit(solution)/shard_map/ppermute | solution.py:31
where the time goes:
time: 140 us; the launch traced here: 139 us
  blocking collectives  79.9 us (57%)
  starting transfers between devices  26.3 us (19%)
  waiting for transfers between devices  20.9 us (15%)
  other arithmetic  5.66 us (4%)
  matrix products  2.84 us (2%)
  local copies, waits for them, and re-layouts  2.81 us (2%)
    all_gather x1, blocking collectives, body(): blocks_all = lax.all_gather(sky_blocks[0].astype(jnp.float32), 'space')  29.6 us
    all_gather x1, blocking collectives, body(): params_all = lax.all_gather(params, 'species')  24.3 us
    ppermute x3, waiting for transfers between devices, from_behind(): return lax.ppermute(block, axis, route)  18 us
    all_gather x1, blocking collectives, body(): gathered = lax.all_gather(contribution, 'space')  17.1 us
    ppermute x2, starting transfers between devices, padded_2(): lax.ppermute(tail, axis, [(i, (i + 1) % count) for i in range(ends)])  13.5 us
    ppermute x3, starting transfers between devices, from_behind(): return lax.ppermute(block, axis, route)  10.3 us
    psum x1, blocking collectives, body(): sums = lax.psum(partial, 'species')  8.89 us
    ppermute x2, waiting for transfers between devices, padded_2(): lax.ppermute(tail, axis, [(i, (i + 1) % count) for i in range(ends)])  2.95 us
  transfers between devices with their start and end apart: 7, of which 3 were waited for; matrix products, arithmetic and copies ran while one was open for 2% of the time, Pallas kernels for 0%

commit v1 on v0

--- a/solution.py
+++ b/solution.py
@@ -83,7 +83,8 @@
     weights = emission_weights(params_all[:, 0], params_all[:, 1], me)
     own_columns = jnp.sum(own_part, axis=3).reshape(bins, -1)
     partial = jnp.dot(weights, own_columns, precision=HIGH, preferred_element_type=jnp.float32)
-    sums = lax.psum(partial, "species")
+    parts = lax.all_gather(partial, "species", axis=0, tiled=False)
+    sums = parts.sum(axis=0)
     emission = (sums / (bins * depth)).astype(jnp.bfloat16).astype(jnp.float32)
     columns = jnp.sum(emission, axis=0)
     contribution = jnp.einsum(

time: 140 us -> 150 us (1.071)
  waiting for transfers between devices: 20.9 us -> 39 us
  blocking collectives: 79.9 us -> 68.4 us
  starting transfers between devices: 26.3 us -> 29.5 us
    ppermute x3, waiting for transfers between devices: 18 us -> 36.1 us  [from_behind(): return lax.ppermute(block, axis, route)]
    all_gather x1, blocking collectives: 24.3 us -> 9.08 us  [body(): params_all = lax.all_gather(params, 'species')]
    all_gather x0 -> x1, blocking collectives: none -> 11.9 us  [body(): parts = lax.all_gather(partial, 'species', axis=0, tiled=False)]
    psum x1 -> x0, blocking collectives: 8.89 us -> none  [body(): sums = lax.psum(partial, 'species')]
    ppermute x3, starting transfers between devices: 10.3 us -> 13.5 us  [from_behind(): return lax.ppermute(block, axis, route)]
  transfers between devices with their start and end apart: 7 -> 7, of which waited for: 3 -> 4; matrix products, arithmetic and copies ran while one was open for 2% -> 2% of each run, Pallas kernels for 0% -> 0%
where the time goes in v1:
time: 150 us; the launch traced here: 149 us
  blocking collectives  68.4 us (46%)
  waiting for transfers between devices  39 us (26%)
  starting transfers between devices  29.5 us (20%)
  other arithmetic  5.68 us (4%)
  matrix products  2.84 us (2%)
  local copies, waits for them, and re-layouts  2.81 us (2%)
    ppermute x3, waiting for transfers between devices, from_behind(): return lax.ppermute(block, axis, route)  36.1 us
    all_gather x1, blocking collectives, body(): blocks_all = lax.all_gather(sky_blocks[0].astype(jnp.float32), 'space')  29.6 us
    all_gather x1, blocking collectives, body(): gathered = lax.all_gather(contribution, 'space')  17.9 us
    ppermute x3, starting transfers between devices, from_behind(): return lax.ppermute(block, axis, route)  13.5 us
    ppermute x2, starting transfers between devices, padded_2(): lax.ppermute(tail, axis, [(i, (i + 1) % count) for i in range(ends)])  13.5 us
    all_gather x1, blocking collectives, body(): parts = lax.all_gather(partial, 'species', axis=0, tiled=False)  11.9 us
    all_gather x1, blocking collectives, body(): params_all = lax.all_gather(params, 'species')  9.08 us
  transfers between devices with their start and end apart: 7, of which 4 were waited for; matrix products, arithmetic and copies ran while one was open for 2% of the time, Pallas kernels for 0%

profile of v1, /device:TPU:0, one launch (start us, length us, event | category | flops | bytes accessed | tf_op | source)
XLA Modules:
  0.0 149.2 jit_solution(12276237256506663535)
XLA Ops:
  0.6 0.0 copy-start
  0.6 0.0 copy-start.1
  0.7 0.0 copy-start.2
  0.7 0.0 copy-start.5
  0.7 1.4 fusion.33
  2.0 1.3 collective-permute-start
  3.4 3.1 %collective-permute-start.1 = (f32[32,1,32,128]{3,2,1,0:T(8,128)S(1)}, f32[32,1,32,128]{3,2,1,0:T(8,128)S(1)}, u32[]{:S(2)}, u32[]{:S(2)}) collective-permute-start(f32[32,1,32,128]{3,2,1,0:T(8,128)S(1)} %get-tuple-element.7), channel_id=1, source_target_pairs={{0,1},{1,2},{2,3},{3,4},{4,5},{5,6},{6,7},{8,9},{9,10},{10,11},{11... | collective-permute-start | bytes 1572872 | tf_op jit(solution)/shard_map/ppermute | solution.py:19
  6.4 0.0 collective-permute-done
  6.4 1.5 collective-permute-done.1
  7.9 0.0 copy-done.1
  7.9 0.0 copy-done.2
  7.9 0.0 copy-done.5
  7.9 0.8 fusion
  8.7 0.1 fusion.32
  8.8 1.3 collective-permute-start.2
  10.1 0.0 copy-start.3
  10.1 10.4 %collective-permute-start.3 = (f32[32,1,32,128]{3,2,1,0:T(8,128)S(1)}, f32[32,1,32,128]{3,2,1,0:T(8,128)S(1)}, u32[]{:S(2)}, u32[]{:S(2)}) collective-permute-start(f32[32,1,32,128]{3,2,1,0:T(8,128)S(1)} %get-tuple-element.5), channel_id=1, source_target_pairs={{0,1},{1,2},{2,3},{3,4},{4,5},{5,6},{6,7},{8,9},{9,10},{10,11},{11... | collective-permute-start | bytes 1572872 | tf_op jit(solution)/shard_map/ppermute | solution.py:19
  20.5 0.0 collective-permute-done.2
  20.5 1.5 collective-permute-done.3
  22.0 0.8 fusion.1
  22.8 0.0 copy-done.3
  22.8 1.7 %convolution_bitcast_fusion = f32[4,8,64,128]{3,1,2,0:T(8,128)S(1)} fusion(f32[4,8,64,128]{3,2,1,0:T(8,128)S(1)} %bitcast.51, f32[1,32,32]{2,1,0:T(8,128)S(1)} %copy-done.3), kind=kOutput, calls=%fused_computation.10 | convolution fusion | flops 100663296 | bytes 2101248 | tf_op jit(solution)/shard_map/dot_general | solution.py:77
  24.5 0.0 copy-start.6
  24.5 0.2 copy.17
  24.7 0.5 copy-done.6
  25.2 0.0 copy-start.4
  25.2 0.5 fusion.31
  25.7 3.6 %collective-permute-start.4 = (f32[32,2,32,128]{3,2,1,0:T(8,128)S(1)}, f32[32,2,32,128]{3,2,1,0:T(8,128)S(1)}, u32[]{:S(2)}, u32[]{:S(2)}) collective-permute-start(f32[32,2,32,128]{3,2,1,0:T(8,128)S(1)} %get-tuple-element.3), channel_id=1, source_target_pairs={{0,8},{8,16},{16,24},{1,9},{9,17},{17,25},{2,10},{10,18},{18,26},{... | collective-permute-start | bytes 3145736 | tf_op jit(solution)/shard_map/ppermute | solution.py:31
  29.2 18.0 %collective-permute-done.4 = f32[32,2,32,128]{3,2,1,0:T(8,128)S(1)} collective-permute-done((f32[32,2,32,128]{3,2,1,0:T(8,128)S(1)}, f32[32,2,32,128]{3,2,1,0:T(8,128)S(1)}, u32[]{:S(2)}, u32[]{:S(2)}) %collective-permute-start.4) | collective-permute-done | bytes 1048608 | tf_op jit(solution)/shard_map/ppermute | solution.py:31
  47.2 0.0 copy-done.4
  47.2 0.0 copy-start.7
  47.2 0.0 copy-start.8
  47.2 0.2 multiply_add_fusion.1
  47.5 5.4 %collective-permute-start.5 = (f32[32,2,32,128]{3,2,1,0:T(8,128)S(1)}, f32[32,2,32,128]{3,2,1,0:T(8,128)}, u32[]{:S(2)}, u32[]{:S(2)}) collective-permute-start(f32[32,2,32,128]{3,2,1,0:T(8,128)S(1)} %multiply_add_fusion.1), channel_id=1, source_target_pairs={{0,8},{8,16},{16,24},{1,9},{9,17},{17,25},{2,10},{10,18},{18,26},{... | collective-permute-start | bytes 3145736 | tf_op jit(solution)/shard_map/ppermute | solution.py:31
  52.8 0.0 copy-done.7
  52.9 0.0 copy-done.8
  52.9 18.1 %collective-permute-done.5 = f32[32,2,32,128]{3,2,1,0:T(8,128)} collective-permute-done((f32[32,2,32,128]{3,2,1,0:T(8,128)S(1)}, f32[32,2,32,128]{3,2,1,0:T(8,128)}, u32[]{:S(2)}, u32[]{:S(2)}) %collective-permute-start.5) | collective-permute-done | bytes 1048608 | tf_op jit(solution)/shard_map/ppermute | solution.py:31
  71.0 1.4 multiply_add_fusion
  72.4 4.6 %collective-permute-start.6 = (f32[32,2,32,128]{3,2,1,0:T(8,128)S(1)}, f32[32,2,32,128]{3,2,1,0:T(8,128)S(1)}, u32[]{:S(2)}, u32[]{:S(2)}) collective-permute-start(f32[32,2,32,128]{3,2,1,0:T(8,128)S(1)} %multiply_add_fusion), channel_id=1, source_target_pairs={{0,8},{8,16},{16,24},{1,9},{9,17},{17,25},{2,10},{10,18},{18,26},{... | collective-permute-start | bytes 3145736 | tf_op jit(solution)/shard_map/ppermute | solution.py:31
  77.0 29.6 %all-gather.3 = f32[8,1,8]{2,1,0:T(1,128)S(1)} all-gather(f32[1,1,8]{2,1,0:T(1,128)S(1)} %convert_bitcast_fusion), channel_id=1, replica_groups=mesh['species'=4,'space'=8] {'space'}, dimensions={0}, use_global_device_ids=true | all-gather | bytes 288 | tf_op jit(solution)/shard_map/all_gather | solution.py:66
  106.6 0.5 broadcast.46
  107.1 0.7 reduce.4
  107.7 0.1 eq.15
  107.8 9.1 %all-gather.4 = f32[4,2,32]{2,1,0:T(2,128)S(1)} all-gather(f32[1,2,32]{2,1,0:T(2,128)S(1)} %maximum_bitcast_fusion), channel_id=2, replica_groups=mesh['species'=4,'space'=8] {'species'}, dimensions={0}, use_global_device_ids=true | all-gather | bytes 1280 | tf_op jit(solution)/shard_map/all_gather | solution.py:65
  116.9 0.1 select_reduce_fusion
  117.0 0.1 reshape.73
  117.1 0.2 convolution_bitcast_fusion.1
  117.3 11.9 %all-gather.5 = f32[4,4,64]{2,1,0:T(4,128)S(1)} all-gather(f32[1,4,64]{2,1,0:T(4,128)S(1)} %convolution_bitcast_fusion.1), channel_id=3, replica_groups=mesh['species'=4,'space'=8] {'species'}, dimensions={0}, use_global_device_ids=true | all-gather | bytes 5120 | tf_op jit(solution)/shard_map/all_gather | solution.py:86
  129.2 0.0 copy-done
  129.2 0.2 fusion.16
  129.3 17.9 %all-gather.2 = f32[64,128]{1,0:T(8,128)S(1)} all-gather(f32[8,128]{1,0:T(8,128)S(1)} %bitcast.52), channel_id=4, replica_groups=mesh['species'=4,'space'=8] {'space'}, dimensions={0}, use_global_device_ids=true | all-gather | bytes 36864 | tf_op jit(solution)/shard_map/all_gather | solution.py:93
  147.2 0.8 fusion.18
  148.0 0.0 collective-permute-done.6
  148.0 1.1 add_bitcast_fusion
  (9 shorter events, 0.1 us)
Async XLA Ops:
  0.6 128.6 %copy-start = (bf16[1,8,64,128]{3,2,1,0:T(8,128)(2,1)S(1)}, bf16[1,8,64,128]{3,2,1,0:T(8,128)(2,1)}, u32[]{:S(2)}) copy-start(bf16[1,8,64,128]{3,2,1,0:T(8,128)(2,1)} %param.16) | copy-start | bytes 393220
  0.6 7.3 %copy-start.1 = (f32[1,32,2,32,128]{4,3,2,1,0:T(8,128)S(1)}, f32[1,32,2,32,128]{4,3,2,1,0:T(8,128)}, u32[]{:S(2)}) copy-start(f32[1,32,2,32,128]{4,3,2,1,0:T(8,128)} %param.9) | copy-start | bytes 3145732
  0.7 7.3 %copy-start.2 = (f32[2,32,128]{2,1,0:T(8,128)S(1)}, f32[2,32,128]{2,1,0:T(8,128)}, u32[]{:S(2)}) copy-start(f32[2,32,128]{2,1,0:T(8,128)} %param.10) | copy-start | bytes 98308
  0.7 7.2 %copy-start.5 = (f32[1,32]{1,0:T(1,128)S(1)}, f32[1,32]{1,0:T(1,128)}, u32[]{:S(2)}) copy-start(f32[1,32]{1,0:T(1,128)} %param.11) | copy-start | bytes 388
  2.0 4.4 %collective-permute-start = (f32[32,1,32,128]{3,2,1,0:T(8,128)S(1)}, f32[32,1,32,128]{3,2,1,0:T(8,128)S(1)}, u32[]{:S(2)}, u32[]{:S(2)}) collective-permute-start(f32[32,1,32,128]{3,2,1,0:T(8,128)S(1)} %get-tuple-element.6), channel_id=1, source_target_pairs={{1,0},{2,1},{3,2},{4,3},{5,4},{6,5},{7,6},{9,8},{10,9},{11,10},{12... | collective-permute-start | bytes 1572872 | tf_op jit(solution)/shard_map/ppermute | solution.py:21
  3.4 4.6 %collective-permute-start.1 = (f32[32,1,32,128]{3,2,1,0:T(8,128)S(1)}, f32[32,1,32,128]{3,2,1,0:T(8,128)S(1)}, u32[]{:S(2)}, u32[]{:S(2)}) collective-permute-start(f32[32,1,32,128]{3,2,1,0:T(8,128)S(1)} %get-tuple-element.7), channel_id=1, source_target_pairs={{0,1},{1,2},{2,3},{3,4},{4,5},{5,6},{6,7},{8,9},{9,10},{10,11},{11... | collective-permute-start | bytes 1572872 | tf_op jit(solution)/shard_map/ppermute | solution.py:19
  8.8 11.7 %collective-permute-start.2 = (f32[32,1,32,128]{3,2,1,0:T(8,128)S(1)}, f32[32,1,32,128]{3,2,1,0:T(8,128)S(1)}, u32[]{:S(2)}, u32[]{:S(2)}) collective-permute-start(f32[32,1,32,128]{3,2,1,0:T(8,128)S(1)} %get-tuple-element.4), channel_id=1, source_target_pairs={{1,0},{2,1},{3,2},{4,3},{5,4},{6,5},{7,6},{9,8},{10,9},{11,10},{12... | collective-permute-start | bytes 1572872 | tf_op jit(solution)/shard_map/ppermute | solution.py:21
  10.1 12.7 %copy-start.3 = (f32[1,32,32]{2,1,0:T(8,128)S(1)}, f32[1,32,32]{2,1,0:T(8,128)}, u32[]{:S(2)}) copy-start(f32[1,32,32]{2,1,0:T(8,128)} %param.12) | copy-start | bytes 12292
  10.1 11.9 %collective-permute-start.3 = (f32[32,1,32,128]{3,2,1,0:T(8,128)S(1)}, f32[32,1,32,128]{3,2,1,0:T(8,128)S(1)}, u32[]{:S(2)}, u32[]{:S(2)}) collective-permute-start(f32[32,1,32,128]{3,2,1,0:T(8,128)S(1)} %get-tuple-element.5), channel_id=1, source_target_pairs={{0,1},{1,2},{2,3},{3,4},{4,5},{5,6},{6,7},{8,9},{9,10},{10,11},{11... | collective-permute-start | bytes 1572872 | tf_op jit(solution)/shard_map/ppermute | solution.py:19
  24.5 0.7 copy-start.6
  25.2 22.0 %copy-start.4 = (f32[1,32]{1,0:T(1,128)S(1)}, f32[1,32]{1,0:T(1,128)}, u32[]{:S(2)}) copy-start(f32[1,32]{1,0:T(1,128)} %param.13) | copy-start | bytes 388
  25.7 21.5 %collective-permute-start.4 = (f32[32,2,32,128]{3,2,1,0:T(8,128)S(1)}, f32[32,2,32,128]{3,2,1,0:T(8,128)S(1)}, u32[]{:S(2)}, u32[]{:S(2)}) collective-permute-start(f32[32,2,32,128]{3,2,1,0:T(8,128)S(1)} %get-tuple-element.3), channel_id=1, source_target_pairs={{0,8},{8,16},{16,24},{1,9},{9,17},{17,25},{2,10},{10,18},{18,26},{... | collective-permute-start | bytes 3145736 | tf_op jit(solution)/shard_map/ppermute | solution.py:31
  47.2 5.6 %copy-start.7 = (f32[1,32]{1,0:T(1,128)S(1)}, f32[1,32]{1,0:T(1,128)}, u32[]{:S(2)}) copy-start(f32[1,32]{1,0:T(1,128)} %param.15) | copy-start | bytes 388
  47.2 5.7 %copy-start.8 = (s32[1,8]{1,0:T(1,128)S(1)}, s32[1,8]{1,0:T(1,128)}, u32[]{:S(2)}) copy-start(s32[1,8]{1,0:T(1,128)} %param.17) | copy-start | bytes 100
  47.5 23.5 %collective-permute-start.5 = (f32[32,2,32,128]{3,2,1,0:T(8,128)S(1)}, f32[32,2,32,128]{3,2,1,0:T(8,128)}, u32[]{:S(2)}, u32[]{:S(2)}) collective-permute-start(f32[32,2,32,128]{3,2,1,0:T(8,128)S(1)} %multiply_add_fusion.1), channel_id=1, source_target_pairs={{0,8},{8,16},{16,24},{1,9},{9,17},{17,25},{2,10},{10,18},{18,26},{... | collective-permute-start | bytes 3145736 | tf_op jit(solution)/shard_map/ppermute | solution.py:31
  72.4 75.7 %collective-permute-start.6 = (f32[32,2,32,128]{3,2,1,0:T(8,128)S(1)}, f32[32,2,32,128]{3,2,1,0:T(8,128)S(1)}, u32[]{:S(2)}, u32[]{:S(2)}) collective-permute-start(f32[32,2,32,128]{3,2,1,0:T(8,128)S(1)} %multiply_add_fusion), channel_id=1, source_target_pairs={{0,8},{8,16},{16,24},{1,9},{9,17},{17,25},{2,10},{10,18},{18,26},{... | collective-permute-start | bytes 3145736 | tf_op jit(solution)/shard_map/ppermute | solution.py:31
